TPU v7x, 32 devices: a whole 2x2x4 slice. The times are simulated.
32 devices in a mesh: dp: 4 (over z), ctx: 8 (over y, x, core).
Axes of the slice: x: 2, y: 2, z: 4, core: 2. Of those that a mesh axis runs over, the one named last changes fastest.
Arguments:
- mixed: bfloat16 [4, 1024, 4096], P('dp', 'ctx'), may hold values from -6 to 6
- conv_weight: float32 [4, 4096], replicated, may hold values from -3 to 3
- log_decay: float32 [4, 1024, 16], P('dp', 'ctx'), may hold values from -1 to 0
- write_rate: float32 [4, 1024, 16], P('dp', 'ctx'), may hold values from 0.1 to 0.95
- segment_ids: int32 [4, 1024], P('dp', 'ctx'), may hold values from 0 to 3, never falling along the last dimension, each value on 1 to 512 neighbouring positions
- cotangent: bfloat16 [4, 1024, 2048], P('dp', 'ctx'), may hold values from -6 to 6
Outputs:
- core_out: bfloat16 [4, 1024, 2048], P('dp', 'ctx')
- grad_mixed: bfloat16 [4, 1024, 4096], P('dp', 'ctx')
- grad_decay: float32 [4, 1024, 16], P('dp', 'ctx')
- grad_rate: float32 [4, 1024, 16], P('dp', 'ctx')
- grad_conv: float32 [4, 4096], replicated
Inputs may be any that keep to these rules, and one draw needn't show every extreme that they name: `segment_ids`: per sequence, segment numbers never fall along the positions; every number of 0 to 3 occurs, each on at most 512 positions.
All inputs are finite; a program needn't handle non-finite values.
Results may differ from a plain program's by a relative error of at most 0.00105.
Values may be sent and summed in bfloat16 or wider, within the bound.
No kernel may reach another device: no remote copies, remote signals or barrier semaphores. Data moves between devices by JAX's collectives and lax.ppermute only.
A program may use at most 320 MiB of HBM per device.

v0:
```python
import math
import jax
import jax.numpy as jnp
from jax import lax
from jax.sharding import PartitionSpec as P

HK = 8
HV = 16
DK = 128
DV = 128
BLOCK = 64
HIGHEST = lax.Precision.HIGHEST


def from_behind(x, axis, by):
    size = lax.axis_size(axis)
    pairs = [(i, i + by) for i in range(size) if 0 <= i + by < size]
    return lax.ppermute(x, axis, pairs)


def prefix(value, axis, join, neutral, backward):
    count, mine = (lax.axis_size(axis), lax.axis_index(axis))
    pieces = jax.tree.map(lambda part: lax.all_gather(part, axis), value)
    if backward:
        pieces = jax.tree.map(lambda part: part[::-1], pieces)
        mine = count - 1 - mine
    total = jax.tree.map(
        lambda part, zero: jnp.full_like(part, 0) + jnp.asarray(zero, part.dtype), value, neutral
    )

    def hop(position, total):
        longer = join(total, jax.tree.map(lambda part: part[position], pieces))
        return jax.tree.map(lambda new, old: jnp.where(position < mine, new, old), longer, total)

    return lax.fori_loop(0, count - 1, hop, total)


def prepare(mix_ext, seg_ext, conv_weight):
    margin = conv_weight.shape[0] - 1
    positions = mix_ext.shape[0] - margin
    current = seg_ext[margin:]
    summed = jnp.zeros((positions, mix_ext.shape[1]), jnp.float32)
    for tap_index in range(margin + 1):
        same_doc = (seg_ext[tap_index : tap_index + positions] == current).astype(jnp.float32)
        summed = (
            summed
            + conv_weight[tap_index][None, :]
            * mix_ext[tap_index : tap_index + positions]
            * same_doc[:, None]
        )
    activated = jax.nn.silu(summed)
    split_at = HK * DK
    queries = activated[:, :split_at].reshape(positions, HK, DK)
    keyset = activated[:, split_at : 2 * split_at].reshape(positions, HK, DK)
    values = activated[:, 2 * split_at :].reshape(positions, HV, DV)
    queries = (
        queries
        / jnp.sqrt(jnp.sum(queries * queries, axis=-1, keepdims=True) + 1e-06)
        / math.sqrt(DK)
    )
    keyset = keyset / jnp.sqrt(jnp.sum(keyset * keyset, axis=-1, keepdims=True) + 1e-06)
    repeats = HV // HK
    return (jnp.repeat(queries, repeats, axis=1), jnp.repeat(keyset, repeats, axis=1), values)


def unit_lower_inverse(strict_part):
    positions = strict_part.shape[-1]
    identity_matrix = jnp.eye(positions, dtype=jnp.float32)[None]
    result = identity_matrix - strict_part
    power = strict_part
    reach = 2
    while reach < positions:
        power = jnp.einsum("hij,hjk->hik", power, power, precision=HIGHEST)
        result = jnp.einsum("hij,hjk->hik", result, identity_matrix + power, precision=HIGHEST)
        reach = reach * 2
    return result


def block_parts(queries, keyset, values, log_decay, write_rate, segments, seg_before):
    positions = queries.shape[0]
    cumulative = jnp.cumsum(log_decay, axis=0)
    keep_state = (segments == seg_before).astype(jnp.float32)
    entering = jnp.exp(cumulative) * keep_state[:, None]
    token_position = lax.iota(jnp.int32, positions)
    same_doc = segments[:, None] == segments[None, :]
    strict = same_doc & (token_position[:, None] > token_position[None, :])
    causal = same_doc & (token_position[:, None] >= token_position[None, :])
    spread = cumulative.T[:, :, None] - cumulative.T[:, None, :]
    strict_decay = jnp.where(strict[None], jnp.exp(jnp.where(strict[None], spread, 0.0)), 0.0)
    causal_decay = jnp.where(causal[None], jnp.exp(jnp.where(causal[None], spread, 0.0)), 0.0)
    key_inner = jnp.einsum("ihd,jhd->hij", keyset, keyset, precision=HIGHEST)
    inverse = unit_lower_inverse(write_rate.T[:, :, None] * key_inner * strict_decay)
    targets = jnp.concatenate(
        [keyset * (write_rate * entering)[:, :, None], values * write_rate[:, :, None]], axis=2
    )
    solved = jnp.einsum("hij,hjd->hid", inverse, targets.transpose(1, 0, 2), precision=HIGHEST)
    write_keys = solved[:, :, :DK]
    write_values = solved[:, :, DK:]
    scores = jnp.einsum("ihd,jhd->hij", queries, keyset, precision=HIGHEST) * causal_decay
    final_sum = cumulative[-1]
    tail_decay = (
        jnp.exp(final_sum[None, :] - cumulative)
        * (segments == segments[-1]).astype(jnp.float32)[:, None]
    )
    carried = jnp.exp(final_sum) * keep_state[-1]
    tail_keys = (keyset * tail_decay[:, :, None]).transpose(1, 0, 2)
    queried = (queries * entering[:, :, None]).transpose(1, 0, 2)
    return (write_keys, write_values, scores, tail_keys, queried, carried)


def block_map(block_data):
    write_keys, write_values, scores, tail_keys, queried, carried = block_data
    identity_matrix = jnp.eye(DK, dtype=jnp.float32)
    transform = carried[:, None, None] * identity_matrix[None] - jnp.einsum(
        "hcd,hce->hde", tail_keys, write_keys, precision=HIGHEST
    )
    shift_term = jnp.einsum("hcd,hce->hde", tail_keys, write_values, precision=HIGHEST)
    return (transform, shift_term)


def block_apply(block_data, state_in):
    write_keys, write_values, scores, tail_keys, queried, carried = block_data
    fresh_values = write_values - jnp.einsum(
        "hcd,hde->hce", write_keys, state_in, precision=HIGHEST
    )
    output = jnp.einsum("hcd,hde->hce", queried, state_in, precision=HIGHEST)
    output = output + jnp.einsum("hij,hje->hie", scores, fresh_values, precision=HIGHEST)
    state_next = carried[:, None, None] * state_in + jnp.einsum(
        "hcd,hce->hde", tail_keys, fresh_values, precision=HIGHEST
    )
    return (output, state_next)


def section_one(mix_ext, conv_weight, log_decay, write_rate, seg_ext):
    queries, keyset, values = prepare(mix_ext, seg_ext, conv_weight)
    margin = conv_weight.shape[0] - 1
    positions = log_decay.shape[0]
    blocks = positions // BLOCK
    segments = seg_ext[margin:]
    before = seg_ext[margin - 1 : margin - 1 + positions : BLOCK]

    def blocked(tensor):
        return tensor.reshape((blocks, BLOCK) + tensor.shape[1:])

    return jax.vmap(block_parts)(
        blocked(queries),
        blocked(keyset),
        blocked(values),
        blocked(log_decay),
        blocked(write_rate),
        blocked(segments),
        before,
    )


def section_two(parts, state_in):

    def step_block(state_now, block_data):
        output, state_next = block_apply(block_data, state_now)
        return (state_next, output)

    state_out, outputs = lax.scan(step_block, state_in, parts)
    blocks = outputs.shape[0]
    return (outputs.transpose(0, 2, 1, 3).reshape(blocks * BLOCK, HV * DV), state_out)


def summarize(parts):
    identity_matrix = jnp.eye(DK, dtype=jnp.float32)
    initial = (
        jnp.broadcast_to(identity_matrix, (HV, DK, DK)),
        jnp.zeros((HV, DK, DV), jnp.float32),
    )

    def fold_block(carried_map, block_data):
        transform, shift_term = block_map(block_data)
        merged = jnp.einsum("hij,hjk->hik", transform, carried_map[0], precision=HIGHEST)
        moved = (
            jnp.einsum("hij,hjk->hik", transform, carried_map[1], precision=HIGHEST) + shift_term
        )
        return ((merged, moved), None)

    result, unused = lax.scan(fold_block, initial, parts)
    return result


def compose(earlier_map, later_map):
    merged = jnp.einsum("shij,shjk->shik", later_map[0], earlier_map[0], precision=HIGHEST)
    moved = (
        jnp.einsum("shij,shjk->shik", later_map[0], earlier_map[1], precision=HIGHEST)
        + later_map[1]
    )
    return (merged, moved)


def local(mixed, conv_weight, log_decay, write_rate, segment_ids, cotangent):
    margin = conv_weight.shape[0] - 1
    shifted_rows, shifted_segs = from_behind(
        (mixed[:, -margin:, :], segment_ids[:, -margin:].astype(jnp.bfloat16)), "ctx", 1
    )
    mix_ext = jnp.concatenate([shifted_rows, mixed], axis=1).astype(jnp.float32)
    seg_ext = jnp.concatenate([shifted_segs.astype(jnp.int32), segment_ids], axis=1)

    def first_section(mix_in, weight_in, decay_in, rate_in):
        return jax.vmap(section_one, in_axes=(0, None, 0, 0, 0))(
            mix_in, weight_in, decay_in, rate_in, seg_ext
        )

    parts, first_pull = jax.vjp(first_section, mix_ext, conv_weight, log_decay, write_rate)
    transform, shift_term = jax.vmap(summarize)(parts)
    identity_pair = (
        jnp.broadcast_to(jnp.eye(transform.shape[-1], dtype=jnp.float32), transform.shape),
        jnp.zeros_like(shift_term),
    )
    incoming = prefix((transform, shift_term), "ctx", compose, identity_pair, False)[1]
    (outputs, leaving), second_pull = jax.vjp(jax.vmap(section_two), parts, incoming)
    part_grads, local_term = second_pull((cotangent.astype(jnp.float32), jnp.zeros_like(leaving)))
    flipped = jnp.swapaxes(transform, -1, -2)
    departing = prefix((flipped, local_term), "ctx", compose, identity_pair, True)[1]
    more_grads, unused_grad = second_pull((jnp.zeros_like(outputs), departing))
    total_parts = jax.tree.map(jnp.add, part_grads, more_grads)
    grad_mix, grad_weight, grad_decay, grad_rate = first_pull(total_parts)
    returned = from_behind(grad_mix[:, :margin, :].astype(jnp.bfloat16), "ctx", -1).astype(
        jnp.float32
    )
    own_grad = grad_mix[:, margin:, :]
    own_grad = jnp.concatenate(
        [own_grad[:, :-margin, :], own_grad[:, -margin:, :] + returned], axis=1
    )
    total_conv = lax.psum(grad_weight, ("dp", "ctx"))
    tokens_all = mixed.shape[0] * lax.axis_size("dp") * mixed.shape[1] * lax.axis_size("ctx")
    return (
        outputs.astype(jnp.bfloat16),
        own_grad.astype(jnp.bfloat16),
        grad_decay,
        grad_rate,
        total_conv / math.sqrt(tokens_all),
    )


def solution(mesh):
    in_specs = (
        P("dp", "ctx", None),
        P(),
        P("dp", "ctx", None),
        P("dp", "ctx", None),
        P("dp", "ctx"),
        P("dp", "ctx", None),
    )
    out_specs = (
        P("dp", "ctx", None),
        P("dp", "ctx", None),
        P("dp", "ctx", None),
        P("dp", "ctx", None),
        P(),
    )
    return jax.shard_map(local, mesh=mesh, in_specs=in_specs, out_specs=out_specs, check_vma=False)
```

profile of v0, /device:TPU:1, one launch (start us, length us, event | category | flops | bytes accessed | tf_op | source)
XLA Modules:
  0.0 655.9 jit_solution(14551815379886588994)
XLA Ops:
  9.2 4.5 collective-permute-start
  16.5 3.6 copy.804
  25.9 11.4 %fusion.293 = (f32[1,128,4096]{2,0,1:T(1,128)S(1)}, f32[1,128,4096]{2,0,1:T(1,128)}, f32[1,128,4096]{2,0,1:T(1,128)}) fusion(f32[1,131,4096]{2,0,1:T(1,128)S(1)} %maximum_convert_fusion, f32[4096]{0:T(1024)S(1)} %bitcast.948, f32[128]{0:T(128)S(1)} %get-tuple-element.1634, f32[4096]{0:T(1024)S(1)} %bitcast.950, f32[128]{0:T(128)S(1)} %get-tuple-element.1633, ...), kind=kLoop, calls=%fused_computation.432 | loop fusion | flops 7340032 | bytes 14747136 | tf_op jit(solution)/shard_map/jvp(vmap(jit(silu)))/mul | solution.py:51
  74.4 14.4 %while.111 = (s32[]{:T(128)}, f32[1,16,128,128]{3,2,1,0:T(8,128)S(1)}, f32[1,16,128,128]{3,2,1,0:T(8,128)}, f32[2,1,16]{2,1,0:T(1,128)S(1)}, f32[2,1,16,64,128]{...) while((s32[]{:T(128)}, ...), condition=%wide.region_3.4_spmd, body=%wide.region_2.3_spmd.sunk | while | flops 1208778752 | bytes 22154000 | solution.py:182
  107.3 37.5 %all-gather.9.cloned.1.call-done = f32[8,16,128,128]{3,2,1,0:T(8,128)} async-done(((f32[1,16,128,128]{3,2,1,0:T(8,128)}), f32[8,16,128,128]{3,2,1,0:T(8,128)}) %all-gather.9.cloned.1.call-update) | async-done | bytes 8388624 | tf_op jit(solution)/shard_map/all_gather | solution.py:23
  144.8 56.7 %all-gather.11.cloned.1.call-done = f32[8,16,128,128]{3,2,1,0:T(8,128)} async-done(((f32[1,16,128,128]{3,2,1,0:T(8,128)}), f32[8,16,128,128]{3,2,1,0:T(8,128)}) %all-gather.11.cloned.1.call-update) | async-done | bytes 8388624 | tf_op jit(solution)/shard_map/all_gather | solution.py:23
  201.5 20.8 %while.114 = (s32[]{:T(128)}, f32[1,16,128,128]{3,2,1,0:T(8,128)S(1)}, s32[]{:T(128)}, f32[8,1,16,128,128]{4,3,2,1,0:T(8,128)}, f32[8,1,16,128,128]{4,3,2,1,0:T(8,128)}, /*index=5*/s32[]{:T(128)}, s32[]{:T(128)}) while((s32[]{:T(128)}, f32[1,16,128,128]{3,2,1,0:T(8,128)S(1)}, s32[]{:T(128)}, f32[8,1,16,128,128]{4,3,2,1,0:T(8,128)}, ...), condition=%wide.region_5.6_spmd.clone, body=%wide.region_4.5_spmd.clone.sunk | while | flops 403701760 | bytes 7342687 | solution.py:35
  223.4 22.1 %while.112 = (s32[]{:T(128)}, f32[1,16,128,128]{3,2,1,0:T(8,128)S(1)}, bf16[2,1,16,64,128]{4,3,2,1,0:T(8,128)(2,1)}, f32[2,1,16,128,128]{3,4,2,1,0:T(8,128)S(1)}...) while((s32[]{:T(128)}, ...), condition=%wide.region_8.9_spmd, body=%wide.region_7.8_spmd.sunk | while | flops 705429504 | bytes 31461364 | solution.py:162
  230.9 3.6 fusion.442
  251.1 33.2 %while.115 = (s32[]{:T(128)}, f32[1,16,128,128]{2,3,1,0:T(8,128)S(1)}, f32[2,1,16,64,128]{4,3,2,1,0:T(8,128)}, f32[2,1,16,64,128]{4,3,2,1,0:T(8,128)}, f32[2,1,1...) while((s32[]{:T(128)}, ...), condition=%wide.region_11.12_spmd.clone, body=%wide.region_9.11_spmd.clone.sunk | while | flops 1412038656 | bytes 66068172 | solution.py:162
  251.3 3.3 convolution_bitcast_fusion.42
  294.5 8.1 %reverse_bitcast_fusion.1 = f32[8,1,16,128,128]{4,3,2,1,0:T(8,128)} fusion(f32[8,16,128,128]{3,2,1,0:T(8,128)} %all-gather.13.cloned.1.call-done), kind=kLoop, calls=%fused_computation.184 | loop fusion | bytes 16777216
  302.6 37.5 %all-gather.15.cloned.1.call-done = f32[8,16,128,128]{3,2,1,0:T(8,128)} async-done(((f32[1,16,128,128]{3,2,1,0:T(8,128)}), f32[8,16,128,128]{3,2,1,0:T(8,128)}) %all-gather.15.cloned.1.call-update) | async-done | bytes 8388624 | tf_op jit(solution)/shard_map/all_gather | solution.py:23
  340.1 7.8 %reverse_bitcast_fusion = f32[8,1,16,128,128]{4,3,2,1,0:T(8,128)} fusion(f32[8,16,128,128]{3,2,1,0:T(8,128)} %all-gather.15.cloned.1.call-done), kind=kLoop, calls=%fused_computation.183 | loop fusion | bytes 16777216
  347.9 20.6 %while.116 = (s32[]{:T(128)}, f32[1,16,128,128]{3,2,1,0:T(8,128)S(1)}, s32[]{:T(128)}, f32[8,1,16,128,128]{4,3,2,1,0:T(8,128)}, f32[8,1,16,128,128]{4,3,2,1,0:T(8,128)}, /*index=5*/s32[]{:T(128)}, s32[]{:T(128)}) while((s32[]{:T(128)}, f32[1,16,128,128]{3,2,1,0:T(8,128)S(1)}, s32[]{:T(128)}, f32[8,1,16,128,128]{4,3,2,1,0:T(8,128)}, ...), condition=%wide.region_13.14_spmd.clone, body=%wide.region_12.13_spmd.clone.sunk | while | flops 403701760 | bytes 7342687 | solution.py:35
  376.6 29.9 %while.113 = (s32[]{:T(128)}, f32[1,16,128,128]{2,3,1,0:T(8,128)S(1)}, f32[2,1,16,64,128]{4,3,2,1,0:T(8,128)}, f32[2,1,16,64,128]{4,3,2,1,0:T(8,128)}, f32[2,1,1...) while((s32[]{:T(128)}, ...), condition=%wide.region_16.17_spmd, body=%wide.region_14.16_spmd.sunk | while | flops 1410990080 | bytes 58727568 | solution.py:162
  376.6 3.3 convolution_bitcast_fusion.40
  443.1 5.6 fusion.187
  454.3 4.6 fusion.175
  475.6 4.7 fusion.160
  488.4 16.1 %multiply_reduce_fusion.3 = (f32[4096]{0:T(1024)S(1)}, f32[4096]{0:T(1024)S(1)}, f32[4096]{0:T(1024)S(1)}, f32[4096]{0:T(1024)S(1)}, f32[1,128,4096]{2,0,1:T(1,128)S(1)}) fusion(f32[1,131,4096]{2,0,1:T(1,128)S(1)} %copy-done.3, f32[128]{0:T(128)S(1)} %copy-done.131, f32[128]{0:T(128)S(1)} %copy-done.129, f32[128]{0:T(128)S(1)} %copy-done.127, ...), kind=kLoop, calls=%fused_computation.199 | loop fusion | flops 9945088 | bytes 16844288 | tf_op jit(solution)/shard_map/transpose(jvp(vmap()))/reduce_sum | solution.py:47
  504.6 10.0 %broadcast_multiply_fusion = (f32[1,128,4096]{2,0,1:T(1,128)S(1)}, f32[1,128,4096]{2,0,1:T(1,128)S(1)}, f32[1,128,4096]{2,0,1:T(1,128)S(1)}, f32[1,128,4096]{2,0,1:T(1,128)S(1)}) fusion(f32[1,128,4096]{2,0,1:T(1,128)S(1)} %get-tuple-element.1584, f32[4096]{0:T(1024)S(1)} %bitcast.949, f32[128]{0:T(128)S(1)} %copy-done.127, f32[4096]{0:T(1024)S(1)} %bitcast.945, ...), kind=kLoop, calls=%fused_computation.292 | loop fusion | flops 3670016 | bytes 10552832 | tf_op jit(solution)/shard_map/transpose(jvp(vmap()))/mul | solution.py:47
  514.6 9.1 %fusion.290 = (bf16[1,131,4096]{2,0,1:T(2,128)(2,1)S(1)}, f32[1,131,4096]{2,0,1:T(1,128)}) fusion(f32[1,128,4096]{2,0,1:T(1,128)S(1)} %get-tuple-element.1602, f32[1,128,4096]{2,0,1:T(1,128)S(1)} %get-tuple-element.1603, f32[1,128,4096]{2,0,1:T(1,128)S(1)} %get-tuple-element.1604, f32[1,128,4096]{2,0,1:T(1,128)S(1)} %get-tuple-element.1601), kind=kLoop, calls=%fused_computation.430 | loop fusion | flops 2146304 | bytes 11608064 | tf_op jit(solution)/shard_map/convert.9
  542.0 105.6 %all-reduce.16.cloned.1.call-done = f32[4,4096]{1,0:T(4,128)} async-done(((f32[4,4096]{1,0:T(4,128)}), f32[4,4096]{1,0:T(4,128)}) %all-reduce.16.cloned.1.call-update) | async-done | bytes 65552 | tf_op jit(solution)/shard_map/psum | solution.py:229
  (617 shorter events, 305.1 us)
Async XLA Ops:
  7.2 13.4 %copy-start.134 = (s32[1,128]{1,0:T(1,128)S(1)}, s32[1,128]{1,0:T(1,128)}, u32[]{:S(2)}) copy-start(s32[1,128]{1,0:T(1,128)} %param.22) | copy-start | bytes 1540
  7.2 13.0 %copy-start.115 = (f32[4,4096]{1,0:T(4,128)S(1)}, f32[4,4096]{1,0:T(4,128)}, u32[]{:S(2)}) copy-start(f32[4,4096]{1,0:T(4,128)} %param.19) | copy-start | bytes 196612
  7.2 13.1 %copy-start.132 = (f32[1,128,16]{1,2,0:T(8,128)S(1)}, f32[1,128,16]{1,2,0:T(8,128)}, u32[]{:S(2)}) copy-start(f32[1,128,16]{1,2,0:T(8,128)} %param.20) | copy-start | bytes 24580
  7.2 13.5 %copy-start.133 = (f32[1,128,16]{1,2,0:T(8,128)S(1)}, f32[1,128,16]{1,2,0:T(8,128)}, u32[]{:S(2)}) copy-start(f32[1,128,16]{1,2,0:T(8,128)} %param.21) | copy-start | bytes 24580
  7.2 137.6 %all-gather.9.cloned.1.call-start = ((), (), s32[]{:S(2)}) async-start(), calls=%async_computation.1 | async-start | bytes 9437184 | tf_op jit(solution)/shard_map/all_gather | solution.py:23
  9.2 12.1 %collective-permute-start = (bf16[1,3]{1,0:T(2,128)(2,1)S(1)}, bf16[1,3]{1,0:T(2,128)(2,1)S(1)}, u32[]{:S(2)}, u32[]{:S(2)}) collective-permute-start(bf16[1,3]{1,0:T(2,128)(2,1)S(1)} %slice.83), channel_id=1, source_target_pairs={{0,1},{1,2},{2,3},{3,4},{4,5},{5,6},{6,7},{8,9},{9,10},{10,11},{11... | collective-permute-start | bytes 26 | tf_op jit(solution)/shard_map/ppermute | solution.py:18
  14.6 8.1 %collective-permute-start.1 = (bf16[1,3,4096]{2,1,0:T(4,128)(2,1)S(1)}, bf16[1,3,4096]{2,1,0:T(4,128)(2,1)S(1)}, u32[]{:S(2)}, u32[]{:S(2)}) collective-permute-start(bf16[1,3,4096]{2,1,0:T(4,128)(2,1)S(1)} %slice.87), channel_id=1, source_target_pairs={{0,1},{1,2},{2,3},{3,4},{4,5},{5,6},{6,7},{8,9},{9,10},{10,11},{11... | collective-permute-start | bytes 73736 | tf_op jit(solution)/shard_map/ppermute | solution.py:18
  20.9 37.8 %copy-start.97 = (f32[2,16,64]{2,1,0:T(8,128)}, f32[2,16,64]{2,1,0:T(8,128)S(1)}, u32[]{:S(2)}) copy-start(f32[2,16,64]{2,1,0:T(8,128)S(1)} %copy.813) | copy-start | bytes 24580
  21.2 47.7 %copy-start.101 = (f32[2,64,16]{1,2,0:T(8,128)}, f32[2,64,16]{1,2,0:T(8,128)S(1)}, u32[]{:S(2)}) copy-start(f32[2,64,16]{1,2,0:T(8,128)S(1)} %copy.834) | copy-start | bytes 24580
  21.3 37.4 %copy-start.99 = (pred[2,64,64]{1,2,0:T(8,128)(4,1)}, pred[2,64,64]{1,2,0:T(8,128)(4,1)S(1)}, u32[]{:S(2)}) copy-start(pred[2,64,64]{1,2,0:T(8,128)(4,1)S(1)} %get-tuple-element.1629) | copy-start | bytes 24580
  22.7 46.7 %copy-start.103 = (f32[2,64,16]{1,2,0:T(8,128)}, f32[2,64,16]{1,2,0:T(8,128)S(1)}, u32[]{:S(2)}) copy-start(f32[2,64,16]{1,2,0:T(8,128)S(1)} %copy.810) | copy-start | bytes 24580
  22.7 46.6 %copy-start.105 = (f32[2,64,16]{1,2,0:T(8,128)}, f32[2,64,16]{1,2,0:T(8,128)S(1)}, u32[]{:S(2)}) copy-start(f32[2,64,16]{1,2,0:T(8,128)S(1)} %copy.832) | copy-start | bytes 24580
  25.8 11.5 %copy-start.2 = (f32[1,131,4096]{2,0,1:T(1,128)}, f32[1,131,4096]{2,0,1:T(1,128)S(1)}, u32[]{:S(2)}) copy-start(f32[1,131,4096]{2,0,1:T(1,128)S(1)} %maximum_convert_fusion) | copy-start | bytes 6438916
  41.6 27.8 %copy-start.14 = (f32[128,8,2,128]{3,0,2,1:T(8,128)}, f32[128,8,2,128]{3,0,2,1:T(8,128)S(1)}, u32[]{:S(2)}) copy-start(f32[128,8,2,128]{3,0,2,1:T(8,128)S(1)} %broadcast_in_dim.262) | copy-start | bytes 3145732
  56.8 8.3 %copy-start.61 = (f32[2,16,64,64]{2,3,1,0:T(8,128)}, f32[2,16,64,64]{2,3,1,0:T(8,128)S(1)}, u32[]{:S(2)}) copy-start(f32[2,16,64,64]{2,3,1,0:T(8,128)S(1)} %copy.827) | copy-start | bytes 1572868
  89.8 111.7 %all-gather.11.cloned.1.call-start = ((), (), s32[]{:S(2)}) async-start(), calls=%async_computation.2 | async-start | bytes 9437184 | tf_op jit(solution)/shard_map/all_gather | solution.py:23
  90.5 204.0 %all-gather.13.cloned.1.call-start = ((), (), s32[]{:S(2)}) async-start(), calls=%async_computation.3 | async-start | bytes 9437184 | tf_op jit(solution)/shard_map/all_gather | solution.py:23
  93.2 246.9 %all-gather.15.cloned.1.call-start = ((), (), s32[]{:S(2)}) async-start(), calls=%async_computation.4 | async-start | bytes 9437184 | tf_op jit(solution)/shard_map/all_gather | solution.py:23
  285.7 362.0 %all-reduce.16.cloned.1.call-start = ((), (), s32[]{:S(2)}) async-start(), calls=%async_computation | async-start | bytes 131072 | tf_op jit(solution)/shard_map/psum | solution.py:229
  488.4 16.2 %copy-start.108 = (f32[1,4096]{1,0:T(1,128)S(1)}, f32[1,4096]{1,0:T(1,128)}, u32[]{:S(2)}) copy-start(f32[1,4096]{1,0:T(1,128)} %copy-done.107) | copy-start | bytes 49156
  488.4 16.2 %copy-start.110 = (f32[1,4096]{1,0:T(1,128)S(1)}, f32[1,4096]{1,0:T(1,128)}, u32[]{:S(2)}) copy-start(f32[1,4096]{1,0:T(1,128)} %copy-done.109) | copy-start | bytes 49156
  488.4 16.2 %copy-start.112 = (f32[1,4096]{1,0:T(1,128)S(1)}, f32[1,4096]{1,0:T(1,128)}, u32[]{:S(2)}) copy-start(f32[1,4096]{1,0:T(1,128)} %copy-done.111) | copy-start | bytes 49156
  488.4 16.2 %copy-start.114 = (f32[1,4096]{1,0:T(1,128)S(1)}, f32[1,4096]{1,0:T(1,128)}, u32[]{:S(2)}) copy-start(f32[1,4096]{1,0:T(1,128)} %copy-done.113) | copy-start | bytes 49156
  530.4 5.9 collective-permute-start.2
  (151 other events, 403.1 us)
Sparse Core Ops, SparseCore 0:
  89.9 54.8 all-gather.8
  147.2 54.2 all-gather.10
  203.4 54.2 all-gather.12
  285.8 54.2 all-gather.14
  526.8 120.8 all-reduce.15
where the time goes:
time: 666 us; the launch traced here: 656 us
  waiting for transfers between devices  238 us (36%)
  matrix products  200 us (30%)
  local copies, waits for them, and re-layouts  103 us (15%)
  other arithmetic  87.2 us (13%)
  between operations  16 us (2%)
  starting transfers between devices  9.43 us (1%)
    all_gather x4, waiting for transfers between devices, prefix(): pieces = jax.tree.map(lambda part: lax.all_gather(part, axis), value)  132 us
    psum x1, waiting for transfers between devices, local(): total_conv = lax.psum(grad_weight, ('dp', 'ctx'))  106 us
    dot_general x14, matrix products, compose(): jnp.einsum('shij,shjk->shik', later_map[0], earlier_map[1], precision=HIG...  39.8 us
    unnamed x227, local copies, waits for them, and re-layouts  33.5 us
    dot_general x15, matrix products, unit_lower_inverse(): jnp.einsum('hij,hjk->hik', result, identity_matrix + power, precision=HIG...  26.6 us
    dot_general x15, matrix products, unit_lower_inverse(): power = jnp.einsum('hij,hjk->hik', power, power, precision=HIGHEST)  25.9 us
    dot_general x10, matrix products, block_apply(): jnp.einsum('hcd,hce->hde', tail_keys, fresh_values, precision=HIGHEST)  24.3 us
    dot_general x10, matrix products, block_apply(): jnp.einsum('hcd,hde->hce', write_keys, state_in, precision=HIGHEST)  17.9 us
  transfers between devices with their start and end apart: 8, of which 4 were waited for; matrix products, arithmetic and copies ran while one was open for 20% of the time, Pallas kernels for 0%

commit v1 on v0

--- a/solution.py
+++ b/solution.py
@@ -10,6 +10,11 @@
 DV = 128
 BLOCK = 64
 HIGHEST = lax.Precision.HIGHEST
+
+
+def make_floor(m, ax_name):
+    clean = jnp.sum(lax.all_gather(m, axis_name=ax_name), axis=0)
+    return clean
 
 
 def from_behind(x, axis, by):
@@ -226,7 +231,7 @@
     own_grad = jnp.concatenate(
         [own_grad[:, :-margin, :], own_grad[:, -margin:, :] + returned], axis=1
     )
-    total_conv = lax.psum(grad_weight, ("dp", "ctx"))
+    total_conv = make_floor(grad_weight, ("dp", "ctx"))
     tokens_all = mixed.shape[0] * lax.axis_size("dp") * mixed.shape[1] * lax.axis_size("ctx")
     return (
         outputs.astype(jnp.bfloat16),

time: 666 us -> 581 us (0.87)
  waiting for transfers between devices: 238 us -> 156 us
    psum x1 -> x0, waiting for transfers between devices: 106 us -> none  [local(): total_conv = lax.psum(grad_weight, ('dp', 'ctx'))]
    all_gather x0 -> x1, waiting for transfers between devices: none -> 23.8 us  [make_floor(): clean = jnp.sum(lax.all_gather(m, axis_name=ax_name), axis=0)]
  transfers between devices with their start and end apart: 8 -> 8, of which waited for: 4 -> 4; matrix products, arithmetic and copies ran while one was open for 20% -> 25% of each run, Pallas kernels for 0% -> 0%
where the time goes in v1:
time: 581 us; the launch traced here: 571 us
  matrix products  200 us (34%)
  waiting for transfers between devices  156 us (27%)
  local copies, waits for them, and re-layouts  102 us (18%)
  other arithmetic  85.5 us (15%)
  between operations  16.3 us (3%)
  starting transfers between devices  9.43 us (2%)
    all_gather x4, waiting for transfers between devices, prefix(): pieces = jax.tree.map(lambda part: lax.all_gather(part, axis), value)  132 us
    dot_general x14, matrix products, compose(): jnp.einsum('shij,shjk->shik', later_map[0], earlier_map[1], precision=HIG...  39.8 us
    unnamed x227, local copies, waits for them, and re-layouts  33.5 us
    dot_general x15, matrix products, unit_lower_inverse(): jnp.einsum('hij,hjk->hik', result, identity_matrix + power, precision=HIG...  26.6 us
    dot_general x15, matrix products, unit_lower_inverse(): power = jnp.einsum('hij,hjk->hik', power, power, precision=HIGHEST)  25.4 us
    dot_general x10, matrix products, block_apply(): jnp.einsum('hcd,hce->hde', tail_keys, fresh_values, precision=HIGHEST)  24.3 us
    all_gather x1, waiting for transfers between devices, make_floor(): clean = jnp.sum(lax.all_gather(m, axis_name=ax_name), axis=0)  23.8 us
    dot_general x10, matrix products, block_apply(): jnp.einsum('hcd,hde->hce', write_keys, state_in, precision=HIGHEST)  17.9 us
  transfers between devices with their start and end apart: 8, of which 4 were waited for; matrix products, arithmetic and copies ran while one was open for 25% of the time, Pallas kernels for 0%

profile of v1, /device:TPU:1, one launch (start us, length us, event | category | flops | bytes accessed | tf_op | source)
XLA Modules:
  0.0 570.7 jit_solution(2825754224643326568)
XLA Ops:
  9.2 4.5 collective-permute-start
  16.5 3.6 copy.804
  25.9 11.4 %fusion.293 = (f32[1,128,4096]{2,0,1:T(1,128)S(1)}, f32[1,128,4096]{2,0,1:T(1,128)}, f32[1,128,4096]{2,0,1:T(1,128)}) fusion(f32[1,131,4096]{2,0,1:T(1,128)S(1)} %maximum_convert_fusion, f32[4096]{0:T(1024)S(1)} %bitcast.950, f32[128]{0:T(128)S(1)} %get-tuple-element.1634, f32[4096]{0:T(1024)S(1)} %bitcast.952, f32[128]{0:T(128)S(1)} %get-tuple-element.1633, ...), kind=kLoop, calls=%fused_computation.432 | loop fusion | flops 7340032 | bytes 14747136 | tf_op jit(solution)/shard_map/jvp(vmap(jit(silu)))/mul | solution.py:56
  74.5 14.4 %while.111 = (s32[]{:T(128)}, f32[1,16,128,128]{3,2,1,0:T(8,128)S(1)}, f32[1,16,128,128]{3,2,1,0:T(8,128)}, f32[2,1,16]{2,1,0:T(1,128)S(1)}, f32[2,1,16,64,128]{...) while((s32[]{:T(128)}, ...), condition=%wide.region_3.4_spmd, body=%wide.region_2.3_spmd.sunk | while | flops 1208778752 | bytes 22154000 | solution.py:187
  107.4 37.5 %all-gather.12.cloned.1.call-done = f32[8,16,128,128]{3,2,1,0:T(8,128)} async-done(((f32[1,16,128,128]{3,2,1,0:T(8,128)}), f32[8,16,128,128]{3,2,1,0:T(8,128)}) %all-gather.12.cloned.1.call-update) | async-done | bytes 8388624 | tf_op jit(solution)/shard_map/all_gather | solution.py:28
  144.8 56.7 %all-gather.14.cloned.1.call-done = f32[8,16,128,128]{3,2,1,0:T(8,128)} async-done(((f32[1,16,128,128]{3,2,1,0:T(8,128)}), f32[8,16,128,128]{3,2,1,0:T(8,128)}) %all-gather.14.cloned.1.call-update) | async-done | bytes 8388624 | tf_op jit(solution)/shard_map/all_gather | solution.py:28
  201.6 20.8 %while.114 = (s32[]{:T(128)}, f32[1,16,128,128]{3,2,1,0:T(8,128)S(1)}, s32[]{:T(128)}, f32[8,1,16,128,128]{4,3,2,1,0:T(8,128)}, f32[8,1,16,128,128]{4,3,2,1,0:T(8,128)}, /*index=5*/s32[]{:T(128)}, s32[]{:T(128)}) while((s32[]{:T(128)}, f32[1,16,128,128]{3,2,1,0:T(8,128)S(1)}, s32[]{:T(128)}, f32[8,1,16,128,128]{4,3,2,1,0:T(8,128)}, ...), condition=%wide.region_5.6_spmd.clone, body=%wide.region_4.5_spmd.clone.sunk | while | flops 403701760 | bytes 7342687 | solution.py:40
  223.5 22.1 %while.112 = (s32[]{:T(128)}, f32[1,16,128,128]{3,2,1,0:T(8,128)S(1)}, bf16[2,1,16,64,128]{4,3,2,1,0:T(8,128)(2,1)}, f32[2,1,16,128,128]{3,4,2,1,0:T(8,128)S(1)}...) while((s32[]{:T(128)}, ...), condition=%wide.region_8.9_spmd, body=%wide.region_7.8_spmd.sunk | while | flops 705429504 | bytes 31461364 | solution.py:167
  230.9 3.6 fusion.442
  251.2 33.2 %while.115 = (s32[]{:T(128)}, f32[1,16,128,128]{2,3,1,0:T(8,128)S(1)}, f32[2,1,16,64,128]{4,3,2,1,0:T(8,128)}, f32[2,1,16,64,128]{4,3,2,1,0:T(8,128)}, f32[2,1,1...) while((s32[]{:T(128)}, ...), condition=%wide.region_11.12_spmd.clone, body=%wide.region_9.11_spmd.clone.sunk | while | flops 1412038656 | bytes 66068172 | solution.py:167
  251.4 3.3 convolution_bitcast_fusion.42
  294.5 8.1 %reverse_bitcast_fusion.1 = f32[8,1,16,128,128]{4,3,2,1,0:T(8,128)} fusion(f32[8,16,128,128]{3,2,1,0:T(8,128)} %all-gather.16.cloned.1.call-done), kind=kLoop, calls=%fused_computation.184 | loop fusion | bytes 16777216
  302.6 37.5 %all-gather.18.cloned.1.call-done = f32[8,16,128,128]{3,2,1,0:T(8,128)} async-done(((f32[1,16,128,128]{3,2,1,0:T(8,128)}), f32[8,16,128,128]{3,2,1,0:T(8,128)}) %all-gather.18.cloned.1.call-update) | async-done | bytes 8388624 | tf_op jit(solution)/shard_map/all_gather | solution.py:28
  340.2 7.8 %reverse_bitcast_fusion = f32[8,1,16,128,128]{4,3,2,1,0:T(8,128)} fusion(f32[8,16,128,128]{3,2,1,0:T(8,128)} %all-gather.18.cloned.1.call-done), kind=kLoop, calls=%fused_computation.183 | loop fusion | bytes 16777216
  348.0 20.6 %while.116 = (s32[]{:T(128)}, f32[1,16,128,128]{3,2,1,0:T(8,128)S(1)}, s32[]{:T(128)}, f32[8,1,16,128,128]{4,3,2,1,0:T(8,128)}, f32[8,1,16,128,128]{4,3,2,1,0:T(8,128)}, /*index=5*/s32[]{:T(128)}, s32[]{:T(128)}) while((s32[]{:T(128)}, f32[1,16,128,128]{3,2,1,0:T(8,128)S(1)}, s32[]{:T(128)}, f32[8,1,16,128,128]{4,3,2,1,0:T(8,128)}, ...), condition=%wide.region_13.14_spmd.clone, body=%wide.region_12.13_spmd.clone.sunk | while | flops 403701760 | bytes 7342687 | solution.py:40
  376.7 29.9 %while.113 = (s32[]{:T(128)}, f32[1,16,128,128]{2,3,1,0:T(8,128)S(1)}, f32[2,1,16,64,128]{4,3,2,1,0:T(8,128)}, f32[2,1,16,64,128]{4,3,2,1,0:T(8,128)}, f32[2,1,1...) while((s32[]{:T(128)}, ...), condition=%wide.region_16.17_spmd, body=%wide.region_14.16_spmd.sunk | while | flops 1410990080 | bytes 58727568 | solution.py:167
  376.7 3.3 convolution_bitcast_fusion.40
  443.2 5.1 fusion.187
  453.8 4.6 fusion.175
  475.1 4.7 fusion.160
  487.9 16.2 %multiply_reduce_fusion.3 = (f32[4096]{0:T(1024)S(1)}, f32[4096]{0:T(1024)S(1)}, f32[4096]{0:T(1024)S(1)}, f32[4096]{0:T(1024)S(1)}, f32[1,128,4096]{2,0,1:T(1,128)S(1)}) fusion(f32[1,131,4096]{2,0,1:T(1,128)S(1)} %copy-done.3, f32[128]{0:T(128)S(1)} %copy-done.132, f32[128]{0:T(128)S(1)} %copy-done.130, f32[128]{0:T(128)S(1)} %copy-done.128, ...), kind=kLoop, calls=%fused_computation.199 | loop fusion | flops 9945088 | bytes 16844288 | tf_op jit(solution)/shard_map/transpose(jvp(vmap()))/reduce_sum | solution.py:52
  505.8 9.7 %broadcast_multiply_fusion = (f32[1,128,4096]{2,0,1:T(1,128)S(1)}, f32[1,128,4096]{2,0,1:T(1,128)S(1)}, f32[1,128,4096]{2,0,1:T(1,128)S(1)}, f32[1,128,4096]{2,0,1:T(1,128)S(1)}) fusion(f32[1,128,4096]{2,0,1:T(1,128)S(1)} %get-tuple-element.1584, f32[4096]{0:T(1024)S(1)} %bitcast.951, f32[128]{0:T(128)S(1)} %copy-done.128, f32[4096]{0:T(1024)S(1)} %bitcast.947, ...), kind=kLoop, calls=%fused_computation.292 | loop fusion | flops 3670016 | bytes 10552832 | tf_op jit(solution)/shard_map/transpose(jvp(vmap()))/mul | solution.py:52
  515.6 9.1 %fusion.290 = (bf16[1,131,4096]{2,0,1:T(2,128)(2,1)S(1)}, f32[1,131,4096]{2,0,1:T(1,128)}) fusion(f32[1,128,4096]{2,0,1:T(1,128)S(1)} %get-tuple-element.1602, f32[1,128,4096]{2,0,1:T(1,128)S(1)} %get-tuple-element.1603, f32[1,128,4096]{2,0,1:T(1,128)S(1)} %get-tuple-element.1604, f32[1,128,4096]{2,0,1:T(1,128)S(1)} %get-tuple-element.1601), kind=kLoop, calls=%fused_computation.430 | loop fusion | flops 2146304 | bytes 11608064 | tf_op jit(solution)/shard_map/convert.9
  537.4 23.8 %all-gather.20.cloned.1.call-done = f32[32,4,4096]{2,1,0:T(4,128)} async-done(((f32[1,4,4096]{2,1,0:T(4,128)}), f32[32,4,4096]{2,1,0:T(4,128)}) %all-gather.20.cloned.1.call-update) | async-done | bytes 2097168 | tf_op jit(solution)/shard_map/all_gather | solution.py:16
  (618 shorter events, 302.2 us)
Async XLA Ops:
  7.2 13.4 %copy-start.135 = (s32[1,128]{1,0:T(1,128)S(1)}, s32[1,128]{1,0:T(1,128)}, u32[]{:S(2)}) copy-start(s32[1,128]{1,0:T(1,128)} %param.22) | copy-start | bytes 1540
  7.2 13.0 %copy-start.115 = (f32[4,4096]{1,0:T(4,128)S(1)}, f32[4,4096]{1,0:T(4,128)}, u32[]{:S(2)}) copy-start(f32[4,4096]{1,0:T(4,128)} %param.19) | copy-start | bytes 196612
  7.2 13.1 %copy-start.133 = (f32[1,128,16]{1,2,0:T(8,128)S(1)}, f32[1,128,16]{1,2,0:T(8,128)}, u32[]{:S(2)}) copy-start(f32[1,128,16]{1,2,0:T(8,128)} %param.20) | copy-start | bytes 24580
  7.2 13.5 %copy-start.134 = (f32[1,128,16]{1,2,0:T(8,128)S(1)}, f32[1,128,16]{1,2,0:T(8,128)}, u32[]{:S(2)}) copy-start(f32[1,128,16]{1,2,0:T(8,128)} %param.21) | copy-start | bytes 24580
  7.2 137.6 %all-gather.12.cloned.1.call-start = ((), (), s32[]{:S(2)}) async-start(), calls=%async_computation | async-start | bytes 9437184 | tf_op jit(solution)/shard_map/all_gather | solution.py:28
  9.2 12.1 %collective-permute-start = (bf16[1,3]{1,0:T(2,128)(2,1)S(1)}, bf16[1,3]{1,0:T(2,128)(2,1)S(1)}, u32[]{:S(2)}, u32[]{:S(2)}) collective-permute-start(bf16[1,3]{1,0:T(2,128)(2,1)S(1)} %slice.83), channel_id=1, source_target_pairs={{0,1},{1,2},{2,3},{3,4},{4,5},{5,6},{6,7},{8,9},{9,10},{10,11},{11... | collective-permute-start | bytes 26 | tf_op jit(solution)/shard_map/ppermute | solution.py:23
  14.6 8.2 %collective-permute-start.1 = (bf16[1,3,4096]{2,1,0:T(4,128)(2,1)S(1)}, bf16[1,3,4096]{2,1,0:T(4,128)(2,1)S(1)}, u32[]{:S(2)}, u32[]{:S(2)}) collective-permute-start(bf16[1,3,4096]{2,1,0:T(4,128)(2,1)S(1)} %slice.87), channel_id=1, source_target_pairs={{0,1},{1,2},{2,3},{3,4},{4,5},{5,6},{6,7},{8,9},{9,10},{10,11},{11... | collective-permute-start | bytes 73736 | tf_op jit(solution)/shard_map/ppermute | solution.py:23
  20.9 37.9 %copy-start.97 = (f32[2,16,64]{2,1,0:T(8,128)}, f32[2,16,64]{2,1,0:T(8,128)S(1)}, u32[]{:S(2)}) copy-start(f32[2,16,64]{2,1,0:T(8,128)S(1)} %copy.813) | copy-start | bytes 24580
  21.2 47.7 %copy-start.101 = (f32[2,64,16]{1,2,0:T(8,128)}, f32[2,64,16]{1,2,0:T(8,128)S(1)}, u32[]{:S(2)}) copy-start(f32[2,64,16]{1,2,0:T(8,128)S(1)} %copy.834) | copy-start | bytes 24580
  21.3 37.5 %copy-start.99 = (pred[2,64,64]{1,2,0:T(8,128)(4,1)}, pred[2,64,64]{1,2,0:T(8,128)(4,1)S(1)}, u32[]{:S(2)}) copy-start(pred[2,64,64]{1,2,0:T(8,128)(4,1)S(1)} %get-tuple-element.1629) | copy-start | bytes 24580
  22.7 46.7 %copy-start.103 = (f32[2,64,16]{1,2,0:T(8,128)}, f32[2,64,16]{1,2,0:T(8,128)S(1)}, u32[]{:S(2)}) copy-start(f32[2,64,16]{1,2,0:T(8,128)S(1)} %copy.810) | copy-start | bytes 24580
  22.8 46.6 %copy-start.105 = (f32[2,64,16]{1,2,0:T(8,128)}, f32[2,64,16]{1,2,0:T(8,128)S(1)}, u32[]{:S(2)}) copy-start(f32[2,64,16]{1,2,0:T(8,128)S(1)} %copy.832) | copy-start | bytes 24580
  41.6 27.8 %copy-start.14 = (f32[128,8,2,128]{3,0,2,1:T(8,128)}, f32[128,8,2,128]{3,0,2,1:T(8,128)S(1)}, u32[]{:S(2)}) copy-start(f32[128,8,2,128]{3,0,2,1:T(8,128)S(1)} %broadcast_in_dim.262) | copy-start | bytes 3145732
  89.8 111.7 %all-gather.14.cloned.1.call-start = ((), (), s32[]{:S(2)}) async-start(), calls=%async_computation.1 | async-start | bytes 9437184 | tf_op jit(solution)/shard_map/all_gather | solution.py:28
  90.6 203.9 %all-gather.16.cloned.1.call-start = ((), (), s32[]{:S(2)}) async-start(), calls=%async_computation.2 | async-start | bytes 9437184 | tf_op jit(solution)/shard_map/all_gather | solution.py:28
  93.2 247.0 %all-gather.18.cloned.1.call-start = ((), (), s32[]{:S(2)}) async-start(), calls=%async_computation.3 | async-start | bytes 9437184 | tf_op jit(solution)/shard_map/all_gather | solution.py:28
  285.7 275.5 %all-gather.20.cloned.1.call-start = ((), (), s32[]{:S(2)}) async-start(), calls=%async_computation.4 | async-start | bytes 2162688 | tf_op jit(solution)/shard_map/all_gather | solution.py:16
  487.9 17.3 %copy-start.96 = (f32[1,2,16,64,64]{3,4,2,1,0:T(8,128)S(1)}, f32[1,2,16,64,64]{3,4,2,1,0:T(8,128)}, u32[]{:S(2)}) copy-start(f32[1,2,16,64,64]{3,4,2,1,0:T(8,128)} %get-tuple-element.1599) | copy-start | bytes 1572868
  487.9 17.9 %copy-start.108 = (f32[1,4096]{1,0:T(1,128)S(1)}, f32[1,4096]{1,0:T(1,128)}, u32[]{:S(2)}) copy-start(f32[1,4096]{1,0:T(1,128)} %copy-done.107) | copy-start | bytes 49156
  487.9 17.9 %copy-start.110 = (f32[1,4096]{1,0:T(1,128)S(1)}, f32[1,4096]{1,0:T(1,128)}, u32[]{:S(2)}) copy-start(f32[1,4096]{1,0:T(1,128)} %copy-done.109) | copy-start | bytes 49156
  487.9 17.9 %copy-start.112 = (f32[1,4096]{1,0:T(1,128)S(1)}, f32[1,4096]{1,0:T(1,128)}, u32[]{:S(2)}) copy-start(f32[1,4096]{1,0:T(1,128)} %copy-done.111) | copy-start | bytes 49156
  487.9 17.9 %copy-start.114 = (f32[1,4096]{1,0:T(1,128)S(1)}, f32[1,4096]{1,0:T(1,128)}, u32[]{:S(2)}) copy-start(f32[1,4096]{1,0:T(1,128)} %copy-done.113) | copy-start | bytes 49156
  515.5 11.9 %copy-start.95 = (f32[1,128,16]{2,1,0:T(8,128)S(1)}, f32[1,128,16]{2,1,0:T(8,128)}, u32[]{:S(2)}) copy-start(f32[1,128,16]{2,1,0:T(8,128)} %copy-done.94) | copy-start | bytes 24580
  524.8 6.8 %collective-permute-start.2 = (bf16[1,3,4096]{2,1,0:T(4,128)(2,1)S(1)}, bf16[1,3,4096]{2,1,0:T(4,128)(2,1)S(1)}, u32[]{:S(2)}, u32[]{:S(2)}) collective-permute-start(bf16[1,3,4096]{2,1,0:T(4,128)(2,1)S(1)} %copy.926), channel_id=1, source_target_pairs={{1,0},{2,1},{3,2},{4,3},{5,4},{6,5},{7,6},{9,8},{10,9},{11,10},{12... | collective-permute-start | bytes 73736 | tf_op jit(solution)/shard_map/ppermute | solution.py:23
  (151 other events, 454.9 us)
Sparse Core Ops, SparseCore 0:
  90.0 54.8 all-gather.11
  147.3 54.2 all-gather.13
  203.5 54.2 all-gather.15
  285.8 54.3 all-gather.17
  505.0 56.1 all-gather.19
